TPU v7x, 512 devices: a whole 4x8x8 slice. The times are simulated.
512 devices in a mesh: req: 64 (over y, z), tp: 8 (over x, core).
Axes of the slice: x: 4, y: 8, z: 8, core: 2. Of those that a mesh axis runs over, the one named last changes fastest.
Arguments:
- hidden_in: bfloat16 [64, 512, 1024], P(None, 'req', 'tp'), may hold values from -64 to 64
- cache_keys: bfloat16 [64, 512, 1024], P('req', None, 'tp'), may hold values from -250 to 250
- cache_values: bfloat16 [64, 512, 1024], P('req', None, 'tp'), may hold values from -6 to 6
- cache_lengths: int32 [64], replicated, may hold values from 32 to 512, as said below
- owner_order: int32 [64], replicated, may hold values from 0 to 63, as said below
- request_slot: int32 [64], replicated, may hold values from 0 to 63, as said below
- proj_weight: bfloat16 [3, 1024, 1024], P(None, None, 'tp'), may hold values from -0.0625 to 0.0625
- proj_bias: bfloat16 [3, 1024], P(None, 'tp'), may hold values from -1.5 to 1.5
- output_weight: bfloat16 [1024, 1024], P('tp'), may hold values from -0.75 to 0.75
- output_bias: bfloat16 [1024], replicated, may hold values from -2.5 to 2.5
- norm_gains: bfloat16 [2, 1024], replicated, may hold values from 0.5 to 1.5
- norm_biases: bfloat16 [2, 1024], replicated, may hold values from -2.5 to 2.5
- widen_weight: bfloat16 [1024, 4096], P(None, 'tp'), may hold values from -0.1875 to 0.1875
- widen_bias: bfloat16 [4096], P('tp'), may hold values from -2.5 to 2.5
- narrow_weight: bfloat16 [4096, 1024], P('tp'), may hold values from -0.09375 to 0.09375
- narrow_bias: bfloat16 [1024], replicated, may hold values from -2.5 to 2.5
Outputs:
- hidden_out: bfloat16 [64, 512, 1024], P(None, 'req', 'tp')
- new_cache: bfloat16 [2, 64, 512, 1024], P(None, 'req', None, 'tp')
Inputs may be any that keep to these rules, and one draw needn't show every extreme that they name: owner_order is a permutation of the requests; owner slot s lies on index s // 1 of req. request_slot[owner_order[s]] = s for every slot s. `cache_lengths`: given in request order; the longest is exactly 512.
All inputs are finite; a program needn't handle non-finite values.
Results may differ from a plain program's by a relative error of at most 0.014.
Values may be sent and summed in bfloat16 or wider, within the bound.
No kernel may reach another device: no remote copies, remote signals or barrier semaphores. Data moves between devices by JAX's collectives and lax.ppermute only.
A program may use at most 64 MiB of HBM per device.

v0:
```python
import jax
import jax.numpy as jnp
from jax import lax
from jax.sharding import PartitionSpec as P

HD = 64


def layer_norm(values, scale_row, shift_row):
    average = jnp.mean(values, axis=-1, keepdims=True)
    centred = values - average
    spread = jnp.mean(centred * centred, axis=-1, keepdims=True)
    return centred * lax.rsqrt(spread + 1e-05) * scale_row.astype(jnp.float32) + shift_row.astype(
        jnp.float32
    )


def split_heads(rows_block):
    return rows_block.reshape(rows_block.shape[0], -1, HD)


def block_scores(query_heads, keys_block, allowed):
    scores = jnp.einsum(
        "thd,shd->hts", query_heads, split_heads(keys_block), preferred_element_type=jnp.float32
    )
    return jnp.where(allowed[None], scores, -jnp.inf)


def to_rows(factor):
    return jnp.transpose(factor, (1, 0, 2))


def slot_attention(fields):
    query_rows, key_rows, value_rows, slot_keys, slot_values, length = fields
    fresh_len = query_rows.shape[0]
    block_len = min(512, slot_keys.shape[0])
    block_count = slot_keys.shape[0] // block_len
    query_heads = split_heads(query_rows)
    self_mask = jnp.arange(fresh_len)[:, None] >= jnp.arange(fresh_len)[None, :]
    self_scores = block_scores(query_heads, key_rows, self_mask)
    row_top = jnp.max(self_scores, axis=2, keepdims=True)
    raised = jnp.exp(self_scores - row_top)
    row_total = jnp.sum(raised, axis=2, keepdims=True)
    context = jnp.einsum(
        "hts,shd->thd",
        raised.astype(jnp.bfloat16),
        split_heads(value_rows),
        preferred_element_type=jnp.float32,
    )
    positions = jnp.arange(block_len)

    def one_block(number, carry):
        old_top, old_total, running = carry
        begin_at = number * block_len
        allowed = jnp.broadcast_to((begin_at + positions < length)[None, :], (fresh_len, block_len))
        scores = block_scores(query_heads, slot_keys, allowed)
        new_top = jnp.maximum(old_top, jnp.max(scores, axis=2, keepdims=True))
        factor = jnp.exp(old_top - new_top)
        block_raised = jnp.exp(scores - new_top)
        new_total = old_total * factor + jnp.sum(block_raised, axis=2, keepdims=True)
        added = jnp.einsum(
            "hts,shd->thd",
            block_raised.astype(jnp.bfloat16),
            split_heads(slot_values),
            preferred_element_type=jnp.float32,
        )
        return (new_top, new_total, running * to_rows(factor) + added)

    row_top, row_total, context = lax.fori_loop(
        0, block_count, one_block, (row_top, row_total, context)
    )
    context = context / to_rows(row_total)
    return context.reshape(fresh_len, -1).astype(jnp.bfloat16)


def widen_rows(normed, widen_weight, widen_bias):
    widened = jnp.dot(normed, widen_weight, preferred_element_type=jnp.float32) + widen_bias.astype(
        jnp.float32
    )
    return jax.nn.gelu(widened, approximate=False).astype(jnp.bfloat16)


def on_device(
    hidden_in,
    cache_keys,
    cache_values,
    cache_lengths,
    owner_order,
    request_slot,
    proj_weight,
    proj_bias,
    output_weight,
    output_bias,
    norm_gains,
    norm_biases,
    widen_weight,
    widen_bias,
    narrow_weight,
    narrow_bias,
):
    slot_count = cache_keys.shape[0]
    fresh_len = hidden_in.shape[1] * lax.axis_size("req")
    owned_slots = lax.dynamic_slice_in_dim(
        owner_order, lax.axis_index("req") * slot_count, slot_count
    )
    lengths = jnp.take(cache_lengths, owned_slots)
    gathered = lax.all_gather(hidden_in, "tp", axis=2, tiled=True)
    token_rows = lax.all_to_all(
        jnp.take(gathered, owner_order, axis=0), "req", split_axis=0, concat_axis=1, tiled=True
    )
    flat_rows = token_rows.reshape(slot_count * fresh_len, -1)
    projected = (
        jnp.einsum("td,cdf->ctf", flat_rows, proj_weight, preferred_element_type=jnp.float32)
        + proj_bias.astype(jnp.float32)[:, None, :]
    )
    query_rows = (
        (projected[0] * HD ** (-0.5)).astype(jnp.bfloat16).reshape(slot_count, fresh_len, -1)
    )
    key_rows = projected[1].astype(jnp.bfloat16).reshape(slot_count, fresh_len, -1)
    value_rows = projected[2].astype(jnp.bfloat16).reshape(slot_count, fresh_len, -1)
    new_cache = jnp.stack([key_rows, value_rows], axis=0)
    context = lax.map(
        slot_attention, (query_rows, key_rows, value_rows, cache_keys, cache_values, lengths)
    )
    context = context.reshape(slot_count * fresh_len, -1)
    tp_count = lax.axis_size("tp")
    attended = lax.psum(
        jnp.dot(context, output_weight, preferred_element_type=jnp.float32).astype(jnp.bfloat16),
        "tp",
    ).astype(jnp.float32)
    normed = layer_norm(
        flat_rows.astype(jnp.float32) + attended + output_bias.astype(jnp.float32),
        norm_gains[0],
        norm_biases[0],
    ).astype(jnp.bfloat16)
    activated = widen_rows(normed, widen_weight, widen_bias)
    fed_total = lax.psum(
        jnp.dot(activated, narrow_weight, preferred_element_type=jnp.float32).astype(jnp.bfloat16),
        "tp",
    ).astype(jnp.float32)
    updated = layer_norm(
        normed.astype(jnp.float32) + fed_total + narrow_bias.astype(jnp.float32),
        norm_gains[1],
        norm_biases[1],
    ).astype(jnp.bfloat16)
    column_count = updated.shape[1] // tp_count
    updated = lax.dynamic_slice_in_dim(
        updated, lax.axis_index("tp") * column_count, column_count, 1
    )
    returned = lax.all_to_all(
        updated.reshape(slot_count, fresh_len, -1), "req", split_axis=1, concat_axis=0, tiled=True
    )
    hidden_out = jnp.take(returned, request_slot, axis=0)
    return (hidden_out, new_cache)


def solution(mesh):
    in_specs = (
        P(None, "req", "tp"),
        P("req", None, "tp"),
        P("req", None, "tp"),
        P(),
        P(),
        P(),
        P(None, None, "tp"),
        P(None, "tp"),
        P("tp", None),
        P(),
        P(),
        P(),
        P(None, "tp"),
        P("tp"),
        P("tp", None),
        P(),
    )
    out_specs = (P(None, "req", "tp"), P(None, "req", None, "tp"))
    return jax.shard_map(
        on_device, mesh=mesh, in_specs=in_specs, out_specs=out_specs, check_vma=False
    )
```

profile of v0, /device:TPU:8, one launch (start us, length us, event | category | flops | bytes accessed | tf_op | source)
XLA Modules:
  0.0 283.8 jit_solution(11562906684038777593)
XLA Ops:
  7.2 0.0 copy-start
  7.2 0.0 all-gather.2.cloned.1.call-start
  7.2 0.7 all-gather.2.cloned.1.call-update
  7.9 0.7 compare_select_fusion
  8.6 0.7 compare_and_fusion
  9.2 34.1 %all-gather.2.cloned.1.call-done = bf16[64,8,1024]{2,1,0:T(8,128)(2,1)} async-done(((bf16[64,8,128]{2,1,0:T(8,128)(2,1)}), bf16[64,8,1024]{2,1,0:T(8,128)(2,1)}) %all-gather.2.cloned.1.call-update) | async-done | bytes 1048592 | tf_op jit(solution)/shard_map/all_gather | solution.py:107
  43.3 1.8 gather_fusion
  45.1 0.0 copy-start.5
  45.2 0.0 copy-start.13
  45.2 1.1 broadcast_select_fusion
  46.3 13.5 %all-to-all-start = ((bf16[64,8,1024]{2,1,0:T(8,128)(2,1)}), bf16[64,8,1024]{2,1,0:T(8,128)(2,1)S(1)}, u32[]{:S(2)}, u32[]{:S(2)}) async-start(bf16[64,8,1024]{2,1,0:T(8,128)(2,1)} %broadcast_select_fusion), calls=%async_computation | async-start | bytes 2097152 | tf_op jit(solution)/shard_map/all_to_all | solution.py:108
  59.8 0.0 all-reduce.3.cloned.1.call-start
  59.9 0.0 copy-done.5
  59.9 0.1 copy.39
  60.0 0.0 copy-done.13
  60.0 0.6 dynamic_slice.20
  62.6 1.4 copy.36
  64.0 0.8 copy.38
  64.8 0.7 dynamic-slice.5
  66.1 0.1 iota_compare_fusion
  66.2 23.3 %all-to-all-done = bf16[64,8,1024]{2,1,0:T(8,128)(2,1)S(1)} async-done(((bf16[64,8,1024]{2,1,0:T(8,128)(2,1)}), bf16[64,8,1024]{2,1,0:T(8,128)(2,1)S(1)}, u32[]{:S(2)}, u32[]{:S(2)}) %all-to-all-start) | async-done | bytes 1048608 | tf_op jit(solution)/shard_map/all_to_all | solution.py:108
  89.5 0.6 fusion.16
  90.1 0.1 add_bitcast_fusion
  90.3 0.1 copy-done.3
  90.4 0.5 select_reduce_fusion
  90.9 0.6 select_reduce_fusion.1
  91.5 0.6 convolution_bitcast_fusion
  92.1 0.9 fusion.2
  93.0 0.0 copy-start.4
  93.0 0.7 fusion.10
  93.7 0.0 copy-start.12
  93.7 0.0 copy-start.7
  93.7 0.0 copy-start.8
  93.7 0.2 copy-done.4
  93.9 1.5 convolution_convert_fusion
  95.4 0.0 all-reduce.3.cloned.1.call-update
  95.4 0.2 all-reduce.5.cloned.1.call-start
  95.7 0.0 copy-done.7
  95.8 68.0 %all-reduce.3.cloned.1.call-done = bf16[512,1024]{1,0:T(8,128)(2,1)} async-done(((bf16[512,1024]{1,0:T(8,128)(2,1)}), bf16[512,1024]{1,0:T(8,128)(2,1)}) %all-reduce.3.cloned.1.call-update) | async-done | bytes 1048592 | tf_op jit(solution)/shard_map/psum | solution.py:127
  163.8 1.7 fusion.6
  165.5 0.6 multiply_reduce_fusion.1
  166.1 0.6 add_convert_fusion
  166.7 0.0 copy-done
  166.7 0.0 copy-start.10
  166.7 0.0 copy-start.15
  166.7 5.6 %convolution_convert_fusion.1 = bf16[512,1024]{1,0:T(8,128)(2,1)} fusion(bf16[512,1024]{1,0:T(8,128)(2,1)S(1)} %copy-done, bf16[512,1024]{1,0:T(8,128)(2,1)S(1)} %add_convert_fusion, bf16[1024,512]{1,0:T(8,128)(2,1)} %param.28, f32[512]{0:T(512)S(1)} %convert_element_type.122), kind=kOutput, calls=%fused_computation.20 | convolution fusion | flops 1091567616 | bytes 4196352 | tf_op jit(solution)/shard_map/dot_general | solution.py:138
  172.4 0.0 all-reduce.5.cloned.1.call-update
  172.4 0.0 copy-done.10
  172.4 0.1 dynamic-slice.7
  172.5 0.1 dynamic-slice.6
  172.6 72.7 %all-reduce.5.cloned.1.call-done = bf16[512,1024]{1,0:T(8,128)(2,1)} async-done(((bf16[512,1024]{1,0:T(8,128)(2,1)}), bf16[512,1024]{1,0:T(8,128)(2,1)}) %all-reduce.5.cloned.1.call-update) | async-done | bytes 1048592 | tf_op jit(solution)/shard_map/psum | solution.py:137
  245.3 1.7 fusion.1
  247.0 0.6 multiply_reduce_fusion
  247.6 0.1 fusion.66
  247.7 0.2 copy.49
  247.9 0.5 broadcast.99
  248.5 1.4 reduce
  249.9 0.7 reshape.238
  250.6 13.4 %all-to-all-start.1 = ((bf16[64,2,512]{2,1,0:T(2,128)(2,1)}), bf16[64,2,512]{2,1,0:T(2,128)(2,1)S(1)}, u32[]{:S(2)}, u32[]{:S(2)}) async-start(bf16[64,2,512]{2,1,0:T(2,128)(2,1)} %reshape.238), calls=%async_computation.1 | async-start | bytes 262144 | tf_op jit(solution)/shard_map/all_to_all | solution.py:150
  264.0 0.8 copy.42
  264.9 10.8 %all-to-all-done.1 = bf16[64,2,512]{2,1,0:T(2,128)(2,1)S(1)} async-done(((bf16[64,2,512]{2,1,0:T(2,128)(2,1)}), bf16[64,2,512]{2,1,0:T(2,128)(2,1)S(1)}, u32[]{:S(2)}, u32[]{:S(2)}) %all-to-all-start.1) | async-done | bytes 131104 | tf_op jit(solution)/shard_map/all_to_all | solution.py:150
  275.7 0.1 reshape.239
  275.8 0.6 gather_fusion.1
  276.5 0.8 broadcast_select_fusion.1
  (37 shorter events, 0.2 us)
Async XLA Ops:
  7.2 159.5 %copy-start = (bf16[512,1024]{1,0:T(8,128)(2,1)S(1)}, bf16[512,1024]{1,0:T(8,128)(2,1)}, u32[]{:S(2)}) copy-start(bf16[512,1024]{1,0:T(8,128)(2,1)} %param.30) | copy-start | bytes 3145732
  7.2 36.1 %all-gather.2.cloned.1.call-start = ((), (), s32[]{:S(2)}) async-start(), calls=%async_computation.2 | async-start | bytes 1179648 | tf_op jit(solution)/shard_map/all_gather | solution.py:107
  45.1 14.7 %copy-start.5 = (bf16[1,512,128]{2,1,0:T(8,128)(2,1)S(1)}, bf16[1,512,128]{2,1,0:T(8,128)(2,1)}, u32[]{:S(2)}) copy-start(bf16[1,512,128]{2,1,0:T(8,128)(2,1)} %param.18) | copy-start | bytes 393220
  45.2 14.9 %copy-start.13 = (s32[64]{0:T(128)S(1)}, s32[64]{0:T(128)}, u32[]{:S(2)}) copy-start(s32[64]{0:T(128)} %param.20) | copy-start | bytes 772
  46.3 17.7 %copy-start.11 = (bf16[3,128]{1,0:T(4,128)(2,1)S(1)}, bf16[3,128]{1,0:T(4,128)(2,1)}, u32[]{:S(2)}) copy-start(bf16[3,128]{1,0:T(4,128)(2,1)} %param.23) | copy-start | bytes 2308
  46.3 17.7 %copy-start.6 = (bf16[1,512,128]{2,1,0:T(8,128)(2,1)S(1)}, bf16[1,512,128]{2,1,0:T(8,128)(2,1)}, u32[]{:S(2)}) copy-start(bf16[1,512,128]{2,1,0:T(8,128)(2,1)} %param.17) | copy-start | bytes 393220
  46.3 18.5 %copy-start.14 = (s32[64]{0:T(128)S(1)}, s32[64]{0:T(128)}, u32[]{:S(2)}) copy-start(s32[64]{0:T(128)} %param.19) | copy-start | bytes 772
  46.3 43.2 %all-to-all-start = ((bf16[64,8,1024]{2,1,0:T(8,128)(2,1)}), bf16[64,8,1024]{2,1,0:T(8,128)(2,1)S(1)}, u32[]{:S(2)}, u32[]{:S(2)}) async-start(bf16[64,8,1024]{2,1,0:T(8,128)(2,1)} %broadcast_select_fusion), calls=%async_computation | async-start | bytes 2097152 | tf_op jit(solution)/shard_map/all_to_all | solution.py:108
  59.8 103.9 %all-reduce.3.cloned.1.call-start = ((), (), s32[]{:S(2)}) async-start(), calls=%async_computation.3 | async-start | bytes 2097152 | tf_op jit(solution)/shard_map/psum | solution.py:127
  89.5 0.9 copy-start.3
  93.0 1.0 copy-start.4
  93.7 2.0 copy-start.9
  93.7 2.0 copy-start.12
  93.7 2.0 copy-start.7
  93.7 2.0 copy-start.8
  95.4 149.8 %all-reduce.5.cloned.1.call-start = ((), (), s32[]{:S(2)}) async-start(), calls=%async_computation.4 | async-start | bytes 2097152 | tf_op jit(solution)/shard_map/psum | solution.py:137
  163.8 1.7 copy-start.1
  166.7 5.7 %copy-start.10 = (bf16[1024]{0:T(1024)(128)(2,1)S(1)}, bf16[1024]{0:T(1024)(128)(2,1)}, u32[]{:S(2)}) copy-start(bf16[1024]{0:T(1024)(128)(2,1)} %param.31) | copy-start | bytes 6148
  166.7 5.9 %copy-start.15 = (s32[64]{0:T(128)S(1)}, s32[64]{0:T(128)}, u32[]{:S(2)}) copy-start(s32[64]{0:T(128)} %param.21) | copy-start | bytes 772
  245.3 1.7 copy-start.2
  250.6 25.1 %all-to-all-start.1 = ((bf16[64,2,512]{2,1,0:T(2,128)(2,1)}), bf16[64,2,512]{2,1,0:T(2,128)(2,1)S(1)}, u32[]{:S(2)}, u32[]{:S(2)}) async-start(bf16[64,2,512]{2,1,0:T(2,128)(2,1)} %reshape.238), calls=%async_computation.1 | async-start | bytes 262144 | tf_op jit(solution)/shard_map/all_to_all | solution.py:150
Sparse Core Ops, SparseCore 0:
  10.1 33.1 all-gather.1
  95.6 68.1 all-reduce.2
  172.5 72.6 all-reduce.4
where the time goes:
time: 284 us
  waiting for transfers between devices  210 us (74%)
  starting transfers between devices  27.2 us (10%)
  between operations  16.8 us (6%)
  other arithmetic  11.2 us (4%)
  matrix products  10 us (4%)
  local copies, waits for them, and re-layouts  8.95 us (3%)
    psum x1, waiting for transfers between devices, on_device(): lax.psum(jnp.dot(activated, narrow_weight, preferred_element_type=jnp.flo...  72.7 us
    psum x1, waiting for transfers between devices, on_device(): lax.psum(jnp.dot(context, output_weight, preferred_element_type=jnp.float...  68 us
    all_gather x1, waiting for transfers between devices, on_device(): gathered = lax.all_gather(hidden_in, 'tp', axis=2, tiled=True)  34.1 us
    all_to_all x1, waiting for transfers between devices, on_device(): lax.all_to_all(jnp.take(gathered, owner_order, axis=0), 'req', split_axis...  23.3 us
    all_to_all x1, starting transfers between devices, on_device(): lax.all_to_all(jnp.take(gathered, owner_order, axis=0), 'req', split_axis...  13.5 us
    all_to_all x1, starting transfers between devices, on_device(): lax.all_to_all(updated.reshape(slot_count, fresh_len, -1), 'req', split_a...  13.4 us
    all_to_all x1, waiting for transfers between devices, on_device(): lax.all_to_all(updated.reshape(slot_count, fresh_len, -1), 'req', split_a...  10.8 us
  transfers between devices with their start and end apart: 5, of which 5 were waited for; matrix products, arithmetic and copies ran while one was open for 2% of the time, Pallas kernels for 0%

commit v1 on v0

--- a/solution.py
+++ b/solution.py
@@ -4,6 +4,22 @@
 from jax.sharding import PartitionSpec as P
 
 HD = 64
+
+
+def ring_gather(x, axis, dim):
+    ways, here, turn = (lax.axis_size(axis), lax.axis_index(axis), x.shape[dim])
+    shape = [n * ways if d == dim else n for d, n in enumerate(x.shape)]
+    full = lax.dynamic_update_slice_in_dim(jnp.zeros(shape, x.dtype), x, here * turn, axis=dim)
+    going_up = going_down = x
+    for far in range(1, ways // 2 + 1):
+        going_up = lax.ppermute(going_up, axis, [(d, (d + 1) % ways) for d in range(ways)])
+        full = lax.dynamic_update_slice_in_dim(full, going_up, (here - far) % ways * turn, axis=dim)
+        if 2 * far < ways:
+            going_down = lax.ppermute(going_down, axis, [(d, (d - 1) % ways) for d in range(ways)])
+            full = lax.dynamic_update_slice_in_dim(
+                full, going_down, (here + far) % ways * turn, axis=dim
+            )
+    return full
 
 
 def layer_norm(values, scale_row, shift_row):
@@ -104,7 +120,7 @@
         owner_order, lax.axis_index("req") * slot_count, slot_count
     )
     lengths = jnp.take(cache_lengths, owned_slots)
-    gathered = lax.all_gather(hidden_in, "tp", axis=2, tiled=True)
+    gathered = ring_gather(hidden_in, "tp", 2)
     token_rows = lax.all_to_all(
         jnp.take(gathered, owner_order, axis=0), "req", split_axis=0, concat_axis=1, tiled=True
     )

time: 284 us -> 268 us (0.944)
  waiting for transfers between devices: 210 us -> 181 us
  starting transfers between devices: 27.2 us -> 39.2 us
    all_gather x1 -> x0, waiting for transfers between devices: 34.1 us -> none  [on_device(): gathered = lax.all_gather(hidden_in, 'tp', axis=2, tiled=True)]
    ppermute x0 -> x7, waiting for transfers between devices: none -> 10.9 us  [the longest x4 10.9 us: ring_gather(): lax.ppermute(going_up, axis, [(d, (d + 1) % ways) for d in range(ways)])]
    ppermute x0 -> x7, starting transfers between devices: none -> 8.88 us  [the longest x3 8.85 us: ring_gather(): lax.ppermute(going_down, axis, [(d, (d - 1) % ways) for d in range(ways)])]
    all_to_all x1, waiting for transfers between devices: 23.3 us -> 19.1 us  [on_device(): lax.all_to_all(jnp.take(gathered, owner_order, axis=0), 'req', split_axis...]
    all_to_all x1, starting transfers between devices: 13.5 us -> 16.7 us  [on_device(): lax.all_to_all(jnp.take(gathered, owner_order, axis=0), 'req', split_axis...]
  transfers between devices with their start and end apart: 5 -> 11, of which waited for: 5 -> 8; matrix products, arithmetic and copies ran while one was open for 2% -> 3% of each run, Pallas kernels for 0% -> 0%
where the time goes in v1:
time: 268 us
  waiting for transfers between devices  181 us (68%)
  starting transfers between devices  39.2 us (15%)
  between operations  17.2 us (6%)
  other arithmetic  11.2 us (4%)
  matrix products  10.1 us (4%)
  local copies, waits for them, and re-layouts  9.01 us (3%)
    psum x1, waiting for transfers between devices, on_device(): lax.psum(jnp.dot(activated, narrow_weight, preferred_element_type=jnp.flo...  72.7 us
    psum x1, waiting for transfers between devices, on_device(): lax.psum(jnp.dot(context, output_weight, preferred_element_type=jnp.float...  67.7 us
    all_to_all x1, waiting for transfers between devices, on_device(): lax.all_to_all(jnp.take(gathered, owner_order, axis=0), 'req', split_axis...  19.1 us
    all_to_all x1, starting transfers between devices, on_device(): lax.all_to_all(jnp.take(gathered, owner_order, axis=0), 'req', split_axis...  16.7 us
    all_to_all x1, starting transfers between devices, on_device(): lax.all_to_all(updated.reshape(slot_count, fresh_len, -1), 'req', split_a...  13.4 us
    ppermute x4, waiting for transfers between devices, ring_gather(): lax.ppermute(going_up, axis, [(d, (d + 1) % ways) for d in range(ways)])  10.9 us
    all_to_all x1, waiting for transfers between devices, on_device(): lax.all_to_all(updated.reshape(slot_count, fresh_len, -1), 'req', split_a...  10.8 us
    ppermute x3, starting transfers between devices, ring_gather(): lax.ppermute(going_down, axis, [(d, (d - 1) % ways) for d in range(ways)])  8.85 us
  transfers between devices with their start and end apart: 11, of which 8 were waited for; matrix products, arithmetic and copies ran while one was open for 3% of the time, Pallas kernels for 0%

profile of v1, /device:TPU:8, one launch (start us, length us, event | category | flops | bytes accessed | tf_op | source)
XLA Modules:
  0.0 268.0 jit_solution(16667191690838985019)
XLA Ops:
  7.2 0.0 copy-start
  7.2 0.0 collective-permute-start
  7.2 2.9 %collective-permute-start.1 = (bf16[64,8,128]{2,1,0:T(8,128)(2,1)}, bf16[64,8,128]{2,1,0:T(8,128)(2,1)S(1)}, u32[]{:S(2)}, u32[]{:S(2)}) collective-permute-start(bf16[64,8,128]{2,1,0:T(8,128)(2,1)} %param.16), channel_id=1, source_target_pairs={{0,7},{1,0},{2,1},{3,2},{4,3},{5,4},{6,5},{7,6},{8,15},{9,8},{10,9... | collective-permute-start | bytes 393224 | tf_op jit(solution)/shard_map/ppermute | solution.py:18
  10.1 0.7 compare_select_fusion
  10.8 0.7 compare_and_fusion
  11.6 0.1 broadcast_in_dim.107
  11.7 0.9 constant_dynamic-update-slice_fusion.7
  12.7 0.3 collective-permute-done
  13.0 3.0 %collective-permute-start.3 = (bf16[64,8,128]{2,1,0:T(8,128)(2,1)S(1)}, bf16[64,8,128]{2,1,0:T(8,128)(2,1)S(1)}, u32[]{:S(2)}, u32[]{:S(2)}) collective-permute-start(bf16[64,8,128]{2,1,0:T(8,128)(2,1)S(1)} %collective-permute-done.1), channel_id=1, source_target_pairs={{0,7},{1,0},{2,1},{3,2},{4,3},{5,4},{6,5},{7,6},{8,15},{9,8},{10,9... | collective-permute-start | bytes 393224 | tf_op jit(solution)/shard_map/ppermute | solution.py:18
  16.1 2.5 collective-permute-done.2
  18.6 3.0 %collective-permute-start.5 = (bf16[64,8,128]{2,1,0:T(8,128)(2,1)S(1)}, bf16[64,8,128]{2,1,0:T(8,128)(2,1)S(1)}, u32[]{:S(2)}, u32[]{:S(2)}) collective-permute-start(bf16[64,8,128]{2,1,0:T(8,128)(2,1)S(1)} %collective-permute-done.3), channel_id=1, source_target_pairs={{0,7},{1,0},{2,1},{3,2},{4,3},{5,4},{6,5},{7,6},{8,15},{9,8},{10,9... | collective-permute-start | bytes 393224 | tf_op jit(solution)/shard_map/ppermute | solution.py:18
  21.7 2.5 collective-permute-done.4
  24.3 5.5 %collective-permute-done.6 = bf16[64,8,128]{2,1,0:T(8,128)(2,1)S(1)} collective-permute-done((bf16[64,8,128]{2,1,0:T(8,128)(2,1)S(1)}, bf16[64,8,128]{2,1,0:T(8,128)(2,1)S(1)}, u32[]{:S(2)}, u32[]{:S(2)}) %collective-permute-start.6) | collective-permute-done | bytes 131104 | tf_op jit(solution)/shard_map/ppermute | solution.py:15
  29.9 0.6 gather_fusion
  30.5 0.0 copy-start.5
  30.5 0.0 copy-start.13
  30.5 1.1 broadcast_select_fusion
  31.6 16.7 %all-to-all-start = ((bf16[64,8,1024]{2,1,0:T(8,128)(2,1)}), bf16[64,8,1024]{2,1,0:T(8,128)(2,1)S(1)}, u32[]{:S(2)}, u32[]{:S(2)}) async-start(bf16[64,8,1024]{2,1,0:T(8,128)(2,1)} %broadcast_select_fusion), calls=%async_computation | async-start | bytes 2097152 | tf_op jit(solution)/shard_map/all_to_all | solution.py:124
  48.4 0.0 all-reduce.3.cloned.1.call-start
  48.4 0.1 copy.39
  48.6 0.6 dynamic_slice.20
  51.1 1.4 copy.36
  52.5 0.8 copy.38
  53.3 0.6 dynamic-slice.5
  54.6 0.1 iota_compare_fusion
  54.6 19.1 %all-to-all-done = bf16[64,8,1024]{2,1,0:T(8,128)(2,1)S(1)} async-done(((bf16[64,8,1024]{2,1,0:T(8,128)(2,1)}), bf16[64,8,1024]{2,1,0:T(8,128)(2,1)S(1)}, u32[]{:S(2)}, u32[]{:S(2)}) %all-to-all-start) | async-done | bytes 1048608 | tf_op jit(solution)/shard_map/all_to_all | solution.py:124
  73.7 0.6 fusion.16
  74.3 0.1 add_bitcast_fusion
  74.5 0.1 copy-done.3
  74.6 0.5 select_reduce_fusion
  75.1 0.6 select_reduce_fusion.1
  75.7 0.6 convolution_bitcast_fusion
  76.3 0.9 fusion.2
  77.2 0.0 copy-start.4
  77.2 0.7 fusion.10
  77.9 0.0 copy-start.12
  77.9 0.0 copy-start.7
  77.9 0.0 copy-start.8
  77.9 0.2 copy-done.4
  78.1 1.5 convolution_convert_fusion
  79.6 0.0 all-reduce.3.cloned.1.call-update
  79.6 0.2 all-reduce.5.cloned.1.call-start
  80.0 67.7 %all-reduce.3.cloned.1.call-done = bf16[512,1024]{1,0:T(8,128)(2,1)} async-done(((bf16[512,1024]{1,0:T(8,128)(2,1)}), bf16[512,1024]{1,0:T(8,128)(2,1)}) %all-reduce.3.cloned.1.call-update) | async-done | bytes 1048592 | tf_op jit(solution)/shard_map/psum | solution.py:143
  147.6 1.7 fusion.6
  149.4 0.6 multiply_reduce_fusion.1
  150.0 0.6 add_convert_fusion
  150.6 5.7 %convolution_convert_fusion.1 = bf16[512,1024]{1,0:T(8,128)(2,1)} fusion(bf16[512,1024]{1,0:T(8,128)(2,1)S(1)} %copy-done, bf16[512,1024]{1,0:T(8,128)(2,1)S(1)} %add_convert_fusion, bf16[1024,512]{1,0:T(8,128)(2,1)} %param.28, f32[512]{0:T(512)S(1)} %convert_element_type.122), kind=kOutput, calls=%fused_computation.20 | convolution fusion | flops 1091567616 | bytes 4196352 | tf_op jit(solution)/shard_map/dot_general | solution.py:154
  156.3 0.0 all-reduce.5.cloned.1.call-update
  156.3 0.1 dynamic-slice.7
  156.4 0.1 dynamic-slice.6
  156.5 72.7 %all-reduce.5.cloned.1.call-done = bf16[512,1024]{1,0:T(8,128)(2,1)} async-done(((bf16[512,1024]{1,0:T(8,128)(2,1)}), bf16[512,1024]{1,0:T(8,128)(2,1)}) %all-reduce.5.cloned.1.call-update) | async-done | bytes 1048592 | tf_op jit(solution)/shard_map/psum | solution.py:153
  229.2 1.7 fusion.1
  230.9 0.6 multiply_reduce_fusion
  231.5 0.1 fusion.66
  231.6 0.2 copy.49
  231.8 0.5 broadcast.106
  232.3 1.4 reduce
  233.8 0.7 reshape.238
  234.5 13.4 %all-to-all-start.1 = ((bf16[64,2,512]{2,1,0:T(2,128)(2,1)}), bf16[64,2,512]{2,1,0:T(2,128)(2,1)S(1)}, u32[]{:S(2)}, u32[]{:S(2)}) async-start(bf16[64,2,512]{2,1,0:T(2,128)(2,1)} %reshape.238), calls=%async_computation.1 | async-start | bytes 262144 | tf_op jit(solution)/shard_map/all_to_all | solution.py:166
  247.9 0.8 copy.42
  248.8 10.8 %all-to-all-done.1 = bf16[64,2,512]{2,1,0:T(2,128)(2,1)S(1)} async-done(((bf16[64,2,512]{2,1,0:T(2,128)(2,1)}), bf16[64,2,512]{2,1,0:T(2,128)(2,1)S(1)}, u32[]{:S(2)}, u32[]{:S(2)}) %all-to-all-start.1) | async-done | bytes 131104 | tf_op jit(solution)/shard_map/all_to_all | solution.py:166
  259.6 0.1 reshape.239
  259.7 0.6 gather_fusion.1
  260.4 0.8 broadcast_select_fusion.1
  (57 shorter events, 0.5 us)
Async XLA Ops:
  7.2 143.4 %copy-start = (bf16[512,1024]{1,0:T(8,128)(2,1)S(1)}, bf16[512,1024]{1,0:T(8,128)(2,1)}, u32[]{:S(2)}) copy-start(bf16[512,1024]{1,0:T(8,128)(2,1)} %param.30) | copy-start | bytes 3145732
  7.2 5.8 %collective-permute-start = (bf16[64,8,128]{2,1,0:T(8,128)(2,1)}, bf16[64,8,128]{2,1,0:T(8,128)(2,1)S(1)}, u32[]{:S(2)}, u32[]{:S(2)}) collective-permute-start(bf16[64,8,128]{2,1,0:T(8,128)(2,1)} %param.16), channel_id=1, source_target_pairs={{0,1},{1,2},{2,3},{3,4},{4,5},{5,6},{6,7},{7,0},{8,9},{9,10},{10,1... | collective-permute-start | bytes 393224 | tf_op jit(solution)/shard_map/ppermute | solution.py:15
  7.2 5.8 %collective-permute-start.1 = (bf16[64,8,128]{2,1,0:T(8,128)(2,1)}, bf16[64,8,128]{2,1,0:T(8,128)(2,1)S(1)}, u32[]{:S(2)}, u32[]{:S(2)}) collective-permute-start(bf16[64,8,128]{2,1,0:T(8,128)(2,1)} %param.16), channel_id=1, source_target_pairs={{0,7},{1,0},{2,1},{3,2},{4,3},{5,4},{6,5},{7,6},{8,15},{9,8},{10,9... | collective-permute-start | bytes 393224 | tf_op jit(solution)/shard_map/ppermute | solution.py:18
  13.0 5.6 %collective-permute-start.2 = (bf16[64,8,128]{2,1,0:T(8,128)(2,1)S(1)}, bf16[64,8,128]{2,1,0:T(8,128)(2,1)S(1)}, u32[]{:S(2)}, u32[]{:S(2)}) collective-permute-start(bf16[64,8,128]{2,1,0:T(8,128)(2,1)S(1)} %collective-permute-done), channel_id=1, source_target_pairs={{0,1},{1,2},{2,3},{3,4},{4,5},{5,6},{6,7},{7,0},{8,9},{9,10},{10,1... | collective-permute-start | bytes 393224 | tf_op jit(solution)/shard_map/ppermute | solution.py:15
  13.0 5.6 %collective-permute-start.3 = (bf16[64,8,128]{2,1,0:T(8,128)(2,1)S(1)}, bf16[64,8,128]{2,1,0:T(8,128)(2,1)S(1)}, u32[]{:S(2)}, u32[]{:S(2)}) collective-permute-start(bf16[64,8,128]{2,1,0:T(8,128)(2,1)S(1)} %collective-permute-done.1), channel_id=1, source_target_pairs={{0,7},{1,0},{2,1},{3,2},{4,3},{5,4},{6,5},{7,6},{8,15},{9,8},{10,9... | collective-permute-start | bytes 393224 | tf_op jit(solution)/shard_map/ppermute | solution.py:18
  18.6 5.6 %collective-permute-start.4 = (bf16[64,8,128]{2,1,0:T(8,128)(2,1)S(1)}, bf16[64,8,128]{2,1,0:T(8,128)(2,1)S(1)}, u32[]{:S(2)}, u32[]{:S(2)}) collective-permute-start(bf16[64,8,128]{2,1,0:T(8,128)(2,1)S(1)} %collective-permute-done.2), channel_id=1, source_target_pairs={{0,1},{1,2},{2,3},{3,4},{4,5},{5,6},{6,7},{7,0},{8,9},{9,10},{10,1... | collective-permute-start | bytes 393224 | tf_op jit(solution)/shard_map/ppermute | solution.py:15
  18.6 5.6 %collective-permute-start.5 = (bf16[64,8,128]{2,1,0:T(8,128)(2,1)S(1)}, bf16[64,8,128]{2,1,0:T(8,128)(2,1)S(1)}, u32[]{:S(2)}, u32[]{:S(2)}) collective-permute-start(bf16[64,8,128]{2,1,0:T(8,128)(2,1)S(1)} %collective-permute-done.3), channel_id=1, source_target_pairs={{0,7},{1,0},{2,1},{3,2},{4,3},{5,4},{6,5},{7,6},{8,15},{9,8},{10,9... | collective-permute-start | bytes 393224 | tf_op jit(solution)/shard_map/ppermute | solution.py:18
  24.2 5.6 %collective-permute-start.6 = (bf16[64,8,128]{2,1,0:T(8,128)(2,1)S(1)}, bf16[64,8,128]{2,1,0:T(8,128)(2,1)S(1)}, u32[]{:S(2)}, u32[]{:S(2)}) collective-permute-start(bf16[64,8,128]{2,1,0:T(8,128)(2,1)S(1)} %collective-permute-done.4), channel_id=1, source_target_pairs={{0,1},{1,2},{2,3},{3,4},{4,5},{5,6},{6,7},{7,0},{8,9},{9,10},{10,1... | collective-permute-start | bytes 393224 | tf_op jit(solution)/shard_map/ppermute | solution.py:15
  30.5 17.9 %copy-start.5 = (bf16[1,512,128]{2,1,0:T(8,128)(2,1)S(1)}, bf16[1,512,128]{2,1,0:T(8,128)(2,1)}, u32[]{:S(2)}) copy-start(bf16[1,512,128]{2,1,0:T(8,128)(2,1)} %param.18) | copy-start | bytes 393220
  30.5 18.1 %copy-start.13 = (s32[64]{0:T(128)S(1)}, s32[64]{0:T(128)}, u32[]{:S(2)}) copy-start(s32[64]{0:T(128)} %param.20) | copy-start | bytes 772
  31.6 20.9 %copy-start.11 = (bf16[3,128]{1,0:T(4,128)(2,1)S(1)}, bf16[3,128]{1,0:T(4,128)(2,1)}, u32[]{:S(2)}) copy-start(bf16[3,128]{1,0:T(4,128)(2,1)} %param.23) | copy-start | bytes 2308
  31.6 20.9 %copy-start.6 = (bf16[1,512,128]{2,1,0:T(8,128)(2,1)S(1)}, bf16[1,512,128]{2,1,0:T(8,128)(2,1)}, u32[]{:S(2)}) copy-start(bf16[1,512,128]{2,1,0:T(8,128)(2,1)} %param.17) | copy-start | bytes 393220
  31.6 21.7 %copy-start.14 = (s32[64]{0:T(128)S(1)}, s32[64]{0:T(128)}, u32[]{:S(2)}) copy-start(s32[64]{0:T(128)} %param.19) | copy-start | bytes 772
  31.6 42.1 %all-to-all-start = ((bf16[64,8,1024]{2,1,0:T(8,128)(2,1)}), bf16[64,8,1024]{2,1,0:T(8,128)(2,1)S(1)}, u32[]{:S(2)}, u32[]{:S(2)}) async-start(bf16[64,8,1024]{2,1,0:T(8,128)(2,1)} %broadcast_select_fusion), calls=%async_computation | async-start | bytes 2097152 | tf_op jit(solution)/shard_map/all_to_all | solution.py:124
  48.4 99.3 %all-reduce.3.cloned.1.call-start = ((), (), s32[]{:S(2)}) async-start(), calls=%async_computation.2 | async-start | bytes 2097152 | tf_op jit(solution)/shard_map/psum | solution.py:143
  73.7 0.9 copy-start.3
  77.2 1.0 copy-start.4
  77.9 2.0 copy-start.9
  77.9 2.0 copy-start.12
  77.9 2.0 copy-start.7
  77.9 2.0 copy-start.8
  79.6 149.5 %all-reduce.5.cloned.1.call-start = ((), (), s32[]{:S(2)}) async-start(), calls=%async_computation.3 | async-start | bytes 2097152 | tf_op jit(solution)/shard_map/psum | solution.py:153
  147.6 1.7 copy-start.1
  150.6 5.7 %copy-start.10 = (bf16[1024]{0:T(1024)(128)(2,1)S(1)}, bf16[1024]{0:T(1024)(128)(2,1)}, u32[]{:S(2)}) copy-start(bf16[1024]{0:T(1024)(128)(2,1)} %param.31) | copy-start | bytes 6148
  150.6 5.9 %copy-start.15 = (s32[64]{0:T(128)S(1)}, s32[64]{0:T(128)}, u32[]{:S(2)}) copy-start(s32[64]{0:T(128)} %param.21) | copy-start | bytes 772
  229.1 1.7 copy-start.2
  234.5 25.1 %all-to-all-start.1 = ((bf16[64,2,512]{2,1,0:T(2,128)(2,1)}), bf16[64,2,512]{2,1,0:T(2,128)(2,1)S(1)}, u32[]{:S(2)}, u32[]{:S(2)}) async-start(bf16[64,2,512]{2,1,0:T(2,128)(2,1)} %reshape.238), calls=%async_computation.1 | async-start | bytes 262144 | tf_op jit(solution)/shard_map/all_to_all | solution.py:166
Sparse Core Ops, SparseCore 0:
  79.8 67.8 all-reduce.2
  156.4 72.6 all-reduce.4
